TPU v7x, 256 devices: a whole 4x4x8 slice. The times are simulated.
256 devices in a mesh: dp: 4 (over x), ctx: 64 (over z, y, core).
Axes of the slice: x: 4, y: 4, z: 8, core: 2. Of those that a mesh axis runs over, the one named last changes fastest.
Arguments:
- inputs: bfloat16 [4, 16384, 2304], P('dp', 'ctx'), may hold values from -16 to 16
- query: bfloat16 [4, 16384, 1024], P('dp', 'ctx'), may hold values from -110 to 110
- w_key: bfloat16 [2304, 512], P('dp'), may hold values from -0.125 to 0.125
- w_value: bfloat16 [2304, 512], P('dp'), may hold values from -0.125 to 0.125
- doc_lengths: int32 [4, 16], P('dp'), may hold values from 1 to 4096, 16384 in all within a row
- grad_out: bfloat16 [4, 16384, 1024], P('dp', 'ctx'), may hold values from -6 to 6
Outputs:
- attended: bfloat16 [4, 16384, 1024], P('dp', 'ctx')
- grad_query: bfloat16 [4, 16384, 1024], P('dp', 'ctx')
- grad_input: bfloat16 [4, 16384, 2304], P('dp', 'ctx')
- grad_wkey: bfloat16 [2304, 512], P('dp')
- grad_wvalue: bfloat16 [2304, 512], P('dp')
All inputs are finite; a program needn't handle non-finite values.
Results may differ from a plain program's by a relative error of at most 0.025.
The roundings to bfloat16 on the way count: a program that leaves them out, or rounds other values in their place, can miss the bound.
Values may be sent and summed in bfloat16 or wider, within the bound.
No kernel may reach another device: no remote copies, remote signals or barrier semaphores. Data moves between devices by JAX's collectives and lax.ppermute only.
A program may use at most 128 MiB of HBM per device.

v0:
```python
import jax
import jax.numpy as jnp
from jax import lax
from jax.sharding import PartitionSpec as P

D = 2304
HQ = 4
HK = 2
HD = 256
WINDOW = 2048
FLOOR = -1e30


def from_behind(value, axis, by):
    peers = lax.axis_size(axis)
    pairs = [(i, i + by) for i in range(peers) if 0 <= i + by < peers]
    return lax.ppermute(value, axis, pairs)


def segment_of(lengths, positions):
    doc_ends = jnp.cumsum(lengths, dtype=jnp.int32)
    return jnp.sum(
        (doc_ends[None, :] <= positions[:, None]).astype(jnp.int32), axis=1, dtype=jnp.int32
    )


def band_mask(query_pos, query_seg, key_pos, key_seg):
    distance_gap = query_pos[:, None] - key_pos[None, :]
    inside = (distance_gap >= 0) & (distance_gap < WINDOW) & (key_pos[None, :] >= 0)
    return inside & (query_seg[:, None] == key_seg[None, :])


def masked_scores(query_heads, key_rows, allowed):
    key_heads = key_rows.reshape(key_rows.shape[0], HK, HD)
    scores = jnp.einsum(
        "qkgd,tkd->kgqt", query_heads, key_heads, preferred_element_type=jnp.float32
    ) * HD ** (-0.5)
    return jnp.where(allowed[None, None], scores, -jnp.inf)


def score_stats(scores):
    highest = jnp.maximum(jnp.max(scores, axis=-1), FLOOR)
    summed = jnp.sum(jnp.exp(scores - highest[..., None]), axis=-1)
    return (highest, summed)


def softmax_of(scores, log_total):
    softmax = jnp.exp(scores - log_total[..., None])
    return (softmax, softmax.astype(jnp.bfloat16))


def values_of(soft_half, value_rows):
    value_heads = value_rows.reshape(value_rows.shape[0], HK, HD)
    return jnp.einsum("kgqt,tkd->qkgd", soft_half, value_heads, preferred_element_type=jnp.float32)


def row_delta(upstream_heads, mixed_half):
    products = upstream_heads.astype(jnp.float32) * mixed_half.astype(jnp.float32)
    return jnp.transpose(jnp.sum(products, axis=-1), (1, 2, 0))


def band_grads(softmax, soft_half, query_heads, upstream_heads, delta_sum, key_rows, value_rows):
    span_rows = key_rows.shape[0]
    key_heads = key_rows.reshape(span_rows, HK, HD)
    value_heads = value_rows.reshape(span_rows, HK, HD)
    prob_grad = jnp.einsum(
        "qkgd,tkd->kgqt", upstream_heads, value_heads, preferred_element_type=jnp.float32
    )
    score_grad = (softmax * (prob_grad - delta_sum[..., None]) * HD ** (-0.5)).astype(jnp.bfloat16)
    query_grad = jnp.einsum(
        "kgqt,tkd->qkgd", score_grad, key_heads, preferred_element_type=jnp.float32
    )
    key_grad = jnp.einsum(
        "kgqt,qkgd->tkd", score_grad, query_heads, preferred_element_type=jnp.float32
    )
    value_grad = jnp.einsum(
        "kgqt,qkgd->tkd", soft_half, upstream_heads, preferred_element_type=jnp.float32
    )
    kv_grad = jnp.concatenate(
        [key_grad.reshape(span_rows, HK * HD), value_grad.reshape(span_rows, HK * HD)], axis=1
    )
    return (query_grad, kv_grad)


def shards(inputs, query, w_key, w_value, doc_lengths, grad_out):
    tokens = inputs[0]
    queries = query[0]
    upstream = grad_out[0]
    lengths = doc_lengths[0]
    tok_rows = tokens.shape[0]
    distant = WINDOW // tok_rows
    per_group = HQ // HK
    kv_width = HK * HD
    key_full, value_full = (
        lax.all_gather(w_key, "dp", axis=0, tiled=True),
        lax.all_gather(w_value, "dp", axis=0, tiled=True),
    )
    key_own = jnp.dot(tokens, key_full, preferred_element_type=jnp.float32).astype(jnp.bfloat16)
    value_own = jnp.dot(tokens, value_full, preferred_element_type=jnp.float32).astype(jnp.bfloat16)
    kv_own = jnp.concatenate([key_own, value_own], axis=1)
    earlier = jnp.concatenate(
        [from_behind(kv_own, "ctx", distance) for distance in range(distant, 0, -1)], axis=0
    )
    window = jnp.concatenate([earlier, kv_own], axis=0)
    device_index = lax.axis_index("ctx")
    first_row = device_index * tok_rows
    query_pos = first_row + jnp.arange(tok_rows, dtype=jnp.int32)
    key_pos = first_row - distant * tok_rows + jnp.arange((distant + 1) * tok_rows, dtype=jnp.int32)
    allowed = band_mask(
        query_pos, segment_of(lengths, query_pos), key_pos, segment_of(lengths, key_pos)
    )
    query_heads = queries.reshape(tok_rows, HK, per_group, HD)
    upstream_heads = upstream.reshape(tok_rows, HK, per_group, HD)
    scores = masked_scores(query_heads, window[:, :kv_width], allowed)
    highest, summed = score_stats(scores)
    log_total = highest + jnp.log(summed)
    softmax, soft_half = softmax_of(scores, log_total)
    mixed_half = values_of(soft_half, window[:, kv_width:]).astype(jnp.bfloat16)
    delta_sum = row_delta(upstream_heads, mixed_half)
    query_grad, window_grad = band_grads(
        softmax,
        soft_half,
        query_heads,
        upstream_heads,
        delta_sum,
        window[:, :kv_width],
        window[:, kv_width:],
    )
    own_grad = window_grad[distant * tok_rows :]
    earlier_grad = window_grad[: distant * tok_rows]
    for distance in range(1, distant + 1):
        lower = (distant - distance) * tok_rows
        own_grad = own_grad + from_behind(earlier_grad[lower : lower + tok_rows], "ctx", -distance)
    kv_grad = own_grad.astype(jnp.bfloat16)
    grad_input = (
        jnp.dot(kv_grad[:, :kv_width], key_full.T, preferred_element_type=jnp.float32)
        + jnp.dot(kv_grad[:, kv_width:], value_full.T, preferred_element_type=jnp.float32)
    ).astype(jnp.bfloat16)
    share_sum = lax.psum_scatter(
        lax.dot_general(
            tokens, kv_grad, (((0,), (0,)), ((), ())), preferred_element_type=jnp.float32
        ),
        "dp",
        scatter_dimension=0,
        tiled=True,
    )
    weight_grad = lax.psum(share_sum, "ctx").astype(jnp.bfloat16)
    attended = mixed_half.reshape(1, tok_rows, HQ * HD)
    grad_query = query_grad.astype(jnp.bfloat16).reshape(1, tok_rows, HQ * HD)
    return (
        attended,
        grad_query,
        grad_input.reshape(1, tok_rows, D),
        weight_grad[:, :kv_width],
        weight_grad[:, kv_width:],
    )


def solution(mesh):
    in_specs = (
        P("dp", "ctx", None),
        P("dp", "ctx", None),
        P("dp", None),
        P("dp", None),
        P("dp", None),
        P("dp", "ctx", None),
    )
    out_specs = (
        P("dp", "ctx", None),
        P("dp", "ctx", None),
        P("dp", "ctx", None),
        P("dp", None),
        P("dp", None),
    )
    return jax.shard_map(shards, mesh=mesh, in_specs=in_specs, out_specs=out_specs, check_vma=False)
```

profile of v0, /device:TPU:2, one launch (start us, length us, event | category | flops | bytes accessed | tf_op | source)
XLA Modules:
  0.0 781.0 jit_solution(336791386545529585)
XLA Ops:
  9.9 37.5 %all-gather.5.cloned.1.call-done = bf16[2304,512]{1,0:T(8,128)(2,1)} async-done(((bf16[576,512]{1,0:T(8,128)(2,1)}), bf16[2304,512]{1,0:T(8,128)(2,1)}) %all-gather.5.cloned.1.call-update) | async-done | bytes 2359312 | tf_op jit(solution)/shard_map/all_gather | solution.py:96
  47.4 2.4 convolution_convert_fusion.1
  49.8 35.0 %all-gather.3.cloned.1.call-done = bf16[2304,512]{1,0:T(8,128)(2,1)} async-done(((bf16[576,512]{1,0:T(8,128)(2,1)}), bf16[2304,512]{1,0:T(8,128)(2,1)}) %all-gather.3.cloned.1.call-update) | async-done | bytes 2359312 | tf_op jit(solution)/shard_map/all_gather | solution.py:95
  84.8 2.4 convolution_convert_fusion.2
  87.3 4.3 collective-permute-start
  91.5 4.4 collective-permute-start.1
  96.0 3.8 collective-permute-start.2
  99.8 3.9 collective-permute-start.3
  103.7 4.6 collective-permute-start.4
  108.3 3.3 fusion.8
  116.0 11.0 %collective-permute-done.1 = bf16[256,1024]{1,0:T(8,128)(2,1)} collective-permute-done((bf16[256,1024]{1,0:T(8,128)(2,1)S(1)}, bf16[256,1024]{1,0:T(8,128)(2,1)}, u32[]{:S(2)}, u32[]{:S(2)}) %collective-permute-start.1) | collective-permute-done | bytes 524320 | tf_op jit(solution)/shard_map/ppermute | solution.py:17
  129.4 9.0 %collective-permute-done.2 = bf16[256,1024]{1,0:T(8,128)(2,1)} collective-permute-done((bf16[256,1024]{1,0:T(8,128)(2,1)S(1)}, bf16[256,1024]{1,0:T(8,128)(2,1)}, u32[]{:S(2)}, u32[]{:S(2)}) %collective-permute-start.2) | collective-permute-done | bytes 524320 | tf_op jit(solution)/shard_map/ppermute | solution.py:17
  143.2 3.2 collective-permute-done.6
  146.5 2.5 fusion.41
  149.0 5.0 reshape.159
  154.0 4.5 copy.84
  158.5 3.8 fusion.43
  163.6 2.7 copy-done.1
  168.5 5.3 fusion.15
  175.8 2.6 multiply_reduce_fusion
  178.3 2.6 fusion.2
  190.8 52.6 %collective-permute-done.15 = f32[256,1024]{0,1:T(8,128)S(1)} collective-permute-done((f32[256,1024]{0,1:T(8,128)S(1)}, f32[256,1024]{0,1:T(8,128)S(1)}, u32[]{:S(2)}, u32[]{:S(2)}) %collective-permute-start.15) | collective-permute-done | bytes 1048608 | tf_op jit(solution)/shard_map/ppermute | solution.py:17
  244.7 13.0 %collective-permute-done.14 = f32[256,1024]{0,1:T(8,128)S(1)} collective-permute-done((f32[256,1024]{0,1:T(8,128)S(1)}, f32[256,1024]{0,1:T(8,128)S(1)}, u32[]{:S(2)}, u32[]{:S(2)}) %collective-permute-start.14) | collective-permute-done | bytes 1048608 | tf_op jit(solution)/shard_map/ppermute | solution.py:17
  260.3 16.9 %collective-permute-done.10 = f32[256,1024]{0,1:T(8,128)S(1)} collective-permute-done((f32[256,1024]{0,1:T(8,128)S(1)}, f32[256,1024]{0,1:T(8,128)S(1)}, u32[]{:S(2)}, u32[]{:S(2)}) %collective-permute-start.10) | collective-permute-done | bytes 1048608 | tf_op jit(solution)/shard_map/ppermute | solution.py:17
  277.3 46.2 %collective-permute-done.9 = f32[256,1024]{0,1:T(8,128)S(1)} collective-permute-done((f32[256,1024]{0,1:T(8,128)S(1)}, f32[256,1024]{0,1:T(8,128)S(1)}, u32[]{:S(2)}, u32[]{:S(2)}) %collective-permute-start.9) | collective-permute-done | bytes 1048608 | tf_op jit(solution)/shard_map/ppermute | solution.py:17
  324.1 5.0 convolution_bitcast_fusion
  329.1 9.6 %copy.98 = f32[2304,1024]{1,0:T(8,128)} copy(f32[2304,1024]{0,1:T(8,128)} %convolution_bitcast_fusion) | data formatting | bytes 18874368
  340.8 4.4 convolution_convert_fusion
  346.2 2.6 fusion.38
  350.7 138.6 %reduce-scatter.4.cloned.1.call-done = f32[576,1024]{1,0:T(8,128)} async-done(((f32[2304,1024]{1,0:T(8,128)}), f32[576,1024]{1,0:T(8,128)}) %reduce-scatter.4.cloned.1.call-update) | async-done | bytes 2359312
  489.3 3.2 copy.99
  492.5 277.9 %all-reduce.1 = bf16[576,1024]{0,1:T(8,128)(2,1)S(1)} all-reduce(f32[576,1024]{0,1:T(8,128)} %copy.99), channel_id=1, replica_groups=mesh['dp'=4,'ctx'=64] {'ctx'}, use_global_device_ids=true, to_apply=%region_7.8 | all-reduce | flops 589824 | bytes 3538944 | tf_op jit(solution)/shard_map/psum | solution.py:147
  (84 shorter events, 43.0 us)
Async XLA Ops:
  7.2 40.2 %copy-start = (bf16[1,256,2304]{2,1,0:T(8,128)(2,1)S(1)}, bf16[1,256,2304]{2,1,0:T(8,128)(2,1)}, u32[]{:S(2)}) copy-start(bf16[1,256,2304]{2,1,0:T(8,128)(2,1)} %param.6) | copy-start | bytes 3538948
  7.2 40.2 %all-gather.5.cloned.1.call-start = ((), (), s32[]{:S(2)}) async-start(), calls=%async_computation.2 | async-start | bytes 2949120 | tf_op jit(solution)/shard_map/all_gather | solution.py:96
  7.9 76.9 %all-gather.3.cloned.1.call-start = ((), (), s32[]{:S(2)}) async-start(), calls=%async_computation.1 | async-start | bytes 2949120 | tf_op jit(solution)/shard_map/all_gather | solution.py:95
  8.7 480.6 %reduce-scatter.4.cloned.1.call-start = ((), (), s32[]{:S(2)}) async-start(), calls=%async_computation.3 | async-start | bytes 11796480
  9.8 101.8 %copy-start.10 = (bf16[1,256,1024]{2,1,0:T(8,128)(2,1)S(1)}, bf16[1,256,1024]{2,1,0:T(8,128)(2,1)}, u32[]{:S(2)}) copy-start(bf16[1,256,1024]{2,1,0:T(8,128)(2,1)} %param.11) | copy-start | bytes 1572868
  9.8 102.8 %copy-start.11 = (bf16[1,256,1024]{2,1,0:T(8,128)(2,1)S(1)}, bf16[1,256,1024]{2,1,0:T(8,128)(2,1)}, u32[]{:S(2)}) copy-start(bf16[1,256,1024]{2,1,0:T(8,128)(2,1)} %param.7) | copy-start | bytes 1572868
  87.3 26.3 %collective-permute-start = (bf16[256,1024]{1,0:T(8,128)(2,1)S(1)}, bf16[256,1024]{1,0:T(8,128)(2,1)}, u32[]{:S(2)}, u32[]{:S(2)}) collective-permute-start(bf16[256,1024]{1,0:T(8,128)(2,1)S(1)} %pad_maximum_fusion.1), channel_id=1, source_target_pairs={{0,8},{1,9},{2,10},{3,11},{4,12},{5,13},{6,14},{7,15},{8,16},{9,17... | collective-permute-start | bytes 1572872 | tf_op jit(solution)/shard_map/ppermute | solution.py:17
  91.5 35.4 %collective-permute-start.1 = (bf16[256,1024]{1,0:T(8,128)(2,1)S(1)}, bf16[256,1024]{1,0:T(8,128)(2,1)}, u32[]{:S(2)}, u32[]{:S(2)}) collective-permute-start(bf16[256,1024]{1,0:T(8,128)(2,1)S(1)} %pad_maximum_fusion.1), channel_id=1, source_target_pairs={{0,7},{1,8},{2,9},{3,10},{4,11},{5,12},{6,13},{7,14},{8,15},{9,16}... | collective-permute-start | bytes 1572872 | tf_op jit(solution)/shard_map/ppermute | solution.py:17
  96.0 42.4 %collective-permute-start.2 = (bf16[256,1024]{1,0:T(8,128)(2,1)S(1)}, bf16[256,1024]{1,0:T(8,128)(2,1)}, u32[]{:S(2)}, u32[]{:S(2)}) collective-permute-start(bf16[256,1024]{1,0:T(8,128)(2,1)S(1)} %pad_maximum_fusion.1), channel_id=1, source_target_pairs={{0,6},{1,7},{2,8},{3,9},{4,10},{5,11},{6,12},{7,13},{8,14},{9,15},... | collective-permute-start | bytes 1572872 | tf_op jit(solution)/shard_map/ppermute | solution.py:17
  99.8 41.2 %collective-permute-start.3 = (bf16[256,1024]{1,0:T(8,128)(2,1)S(1)}, bf16[256,1024]{1,0:T(8,128)(2,1)}, u32[]{:S(2)}, u32[]{:S(2)}) collective-permute-start(bf16[256,1024]{1,0:T(8,128)(2,1)S(1)} %pad_maximum_fusion.1), channel_id=1, source_target_pairs={{0,5},{1,6},{2,7},{3,8},{4,9},{5,10},{6,11},{7,12},{8,13},{9,14},{... | collective-permute-start | bytes 1572872 | tf_op jit(solution)/shard_map/ppermute | solution.py:17
  103.7 38.3 %collective-permute-start.4 = (bf16[256,1024]{1,0:T(8,128)(2,1)S(1)}, bf16[256,1024]{1,0:T(8,128)(2,1)}, u32[]{:S(2)}, u32[]{:S(2)}) collective-permute-start(bf16[256,1024]{1,0:T(8,128)(2,1)S(1)} %pad_maximum_fusion.1), channel_id=1, source_target_pairs={{0,4},{1,5},{2,6},{3,7},{4,8},{5,9},{6,10},{7,11},{8,12},{9,13},{1... | collective-permute-start | bytes 1572872 | tf_op jit(solution)/shard_map/ppermute | solution.py:17
  113.6 29.5 %collective-permute-start.5 = (bf16[256,1024]{1,0:T(8,128)(2,1)S(1)}, bf16[256,1024]{1,0:T(8,128)(2,1)S(1)}, u32[]{:S(2)}, u32[]{:S(2)}) collective-permute-start(bf16[256,1024]{1,0:T(8,128)(2,1)S(1)} %pad_maximum_fusion.1), channel_id=1, source_target_pairs={{0,3},{1,4},{2,5},{3,6},{4,7},{5,8},{6,9},{7,10},{8,11},{9,12},{10... | collective-permute-start | bytes 1572872 | tf_op jit(solution)/shard_map/ppermute | solution.py:17
  127.0 19.4 %collective-permute-start.6 = (bf16[256,1024]{1,0:T(8,128)(2,1)S(1)}, bf16[256,1024]{1,0:T(8,128)(2,1)S(1)}, u32[]{:S(2)}, u32[]{:S(2)}) collective-permute-start(bf16[256,1024]{1,0:T(8,128)(2,1)S(1)} %pad_maximum_fusion.1), channel_id=1, source_target_pairs={{0,2},{1,3},{2,4},{3,5},{4,6},{5,7},{6,8},{7,9},{8,10},{9,11},{10,... | collective-permute-start | bytes 1572872 | tf_op jit(solution)/shard_map/ppermute | solution.py:17
  138.3 8.1 %collective-permute-start.7 = (bf16[256,1024]{1,0:T(8,128)(2,1)S(1)}, bf16[256,1024]{1,0:T(8,128)(2,1)S(1)}, u32[]{:S(2)}, u32[]{:S(2)}) collective-permute-start(bf16[256,1024]{1,0:T(8,128)(2,1)S(1)} %pad_maximum_fusion.1), channel_id=1, source_target_pairs={{0,1},{1,2},{2,3},{3,4},{4,5},{5,6},{6,7},{7,8},{8,9},{9,10},{10,1... | collective-permute-start | bytes 1572872 | tf_op jit(solution)/shard_map/ppermute | solution.py:17
  162.4 4.0 copy-start.1
  162.4 4.0 copy-start.3
  168.5 6.5 copy-start.2
  168.5 7.2 copy-start.6
  168.5 7.2 copy-start.8
  175.8 2.6 copy-start.9
  178.3 2.6 copy-start.7
  181.0 2.2 copy-start.4
  184.1 59.4 %collective-permute-start.15 = (f32[256,1024]{0,1:T(8,128)S(1)}, f32[256,1024]{0,1:T(8,128)S(1)}, u32[]{:S(2)}, u32[]{:S(2)}) collective-permute-start(f32[256,1024]{0,1:T(8,128)S(1)} %get-tuple-element.31), channel_id=1, source_target_pairs={{8,0},{9,1},{10,2},{11,3},{12,4},{13,5},{14,6},{15,7},{16,8},{17,9... | collective-permute-start | bytes 3145736 | tf_op jit(solution)/shard_map/ppermute | solution.py:17
  185.4 72.3 %collective-permute-start.14 = (f32[256,1024]{0,1:T(8,128)S(1)}, f32[256,1024]{0,1:T(8,128)S(1)}, u32[]{:S(2)}, u32[]{:S(2)}) collective-permute-start(f32[256,1024]{0,1:T(8,128)S(1)} %get-tuple-element.32), channel_id=1, source_target_pairs={{7,0},{8,1},{9,2},{10,3},{11,4},{12,5},{13,6},{14,7},{15,8},{16,9}... | collective-permute-start | bytes 3145736 | tf_op jit(solution)/shard_map/ppermute | solution.py:17
  186.7 72.3 %collective-permute-start.13 = (f32[256,1024]{0,1:T(8,128)S(1)}, f32[256,1024]{0,1:T(8,128)S(1)}, u32[]{:S(2)}, u32[]{:S(2)}) collective-permute-start(f32[256,1024]{0,1:T(8,128)S(1)} %get-tuple-element.30), channel_id=1, source_target_pairs={{6,0},{7,1},{8,2},{9,3},{10,4},{11,5},{12,6},{13,7},{14,8},{15,9},... | collective-permute-start | bytes 3145736 | tf_op jit(solution)/shard_map/ppermute | solution.py:17
  188.2 72.1 %collective-permute-start.12 = (f32[256,1024]{0,1:T(8,128)S(1)}, f32[256,1024]{0,1:T(8,128)S(1)}, u32[]{:S(2)}, u32[]{:S(2)}) collective-permute-start(f32[256,1024]{0,1:T(8,128)S(1)} %get-tuple-element.29), channel_id=1, source_target_pairs={{5,0},{6,1},{7,2},{8,3},{9,4},{10,5},{11,6},{12,7},{13,8},{14,9},{... | collective-permute-start | bytes 3145736 | tf_op jit(solution)/shard_map/ppermute | solution.py:17
  189.5 70.8 %collective-permute-start.11 = (f32[256,1024]{0,1:T(8,128)S(1)}, f32[256,1024]{0,1:T(8,128)S(1)}, u32[]{:S(2)}, u32[]{:S(2)}) collective-permute-start(f32[256,1024]{0,1:T(8,128)S(1)} %get-tuple-element.28), channel_id=1, source_target_pairs={{4,0},{5,1},{6,2},{7,3},{8,4},{9,5},{10,6},{11,7},{12,8},{13,9},{1... | collective-permute-start | bytes 3145736 | tf_op jit(solution)/shard_map/ppermute | solution.py:17
  243.4 33.8 %collective-permute-start.10 = (f32[256,1024]{0,1:T(8,128)S(1)}, f32[256,1024]{0,1:T(8,128)S(1)}, u32[]{:S(2)}, u32[]{:S(2)}) collective-permute-start(f32[256,1024]{0,1:T(8,128)S(1)} %get-tuple-element.27), channel_id=1, source_target_pairs={{3,0},{4,1},{5,2},{6,3},{7,4},{8,5},{9,6},{10,7},{11,8},{12,9},{13... | collective-permute-start | bytes 3145736 | tf_op jit(solution)/shard_map/ppermute | solution.py:17
  257.7 65.7 %collective-permute-start.9 = (f32[256,1024]{0,1:T(8,128)S(1)}, f32[256,1024]{0,1:T(8,128)S(1)}, u32[]{:S(2)}, u32[]{:S(2)}) collective-permute-start(f32[256,1024]{0,1:T(8,128)S(1)} %get-tuple-element.26), channel_id=1, source_target_pairs={{2,0},{3,1},{4,2},{5,3},{6,4},{7,5},{8,6},{9,7},{10,8},{11,9},{12,... | collective-permute-start | bytes 3145736 | tf_op jit(solution)/shard_map/ppermute | solution.py:17
  259.0 64.4 %collective-permute-start.8 = (f32[256,1024]{0,1:T(8,128)S(1)}, f32[256,1024]{0,1:T(8,128)S(1)}, u32[]{:S(2)}, u32[]{:S(2)}) collective-permute-start(f32[256,1024]{0,1:T(8,128)S(1)} %get-tuple-element.25), channel_id=1, source_target_pairs={{1,0},{2,1},{3,2},{4,3},{5,4},{6,5},{7,6},{8,7},{9,8},{10,9},{11,1... | collective-permute-start | bytes 3145736 | tf_op jit(solution)/shard_map/ppermute | solution.py:17
  338.7 1.0 copy-start.12
  346.2 2.6 copy-start.5
Sparse Core Ops, SparseCore 0:
  9.8 37.5 all-gather.4
  49.2 35.5 all-gather.2
  338.9 150.3 reduce-scatter.3
where the time goes:
time: 782 us; the launch traced here: 781 us
  waiting for transfers between devices  364 us (47%)
  blocking collectives  278 us (36%)
  local copies, waits for them, and re-layouts  47.8 us (6%)
  starting transfers between devices  35.8 us (5%)
  matrix products  34.5 us (4%)
  between operations  14.2 us (2%)
    psum x1, blocking collectives, shards(): weight_grad = lax.psum(share_sum, 'ctx').astype(jnp.bfloat16)  278 us
    ppermute x16, waiting for transfers between devices, from_behind(): return lax.ppermute(value, axis, pairs)  152 us
    unnamed x4, waiting for transfers between devices  140 us
    all_gather x1, waiting for transfers between devices, shards(): lax.all_gather(w_value, 'dp', axis=0, tiled=True)  37.5 us
    ppermute x16, starting transfers between devices, from_behind(): return lax.ppermute(value, axis, pairs)  35.7 us
    all_gather x1, waiting for transfers between devices, shards(): lax.all_gather(w_key, 'dp', axis=0, tiled=True)  35 us
    unnamed x41, local copies, waits for them, and re-layouts  30.9 us
  transfers between devices with their start and end apart: 19, of which 10 were waited for; matrix products, arithmetic and copies ran while one was open for 3% of the time, Pallas kernels for 0%

commit v1 on v0

--- a/solution.py
+++ b/solution.py
@@ -9,6 +9,28 @@
 HD = 256
 WINDOW = 2048
 FLOOR = -1e30
+
+
+def laid_out(blocks, dim):
+    blocks = jnp.moveaxis(blocks, 0, dim)
+    dims = blocks.shape
+    return blocks.reshape(*dims[:dim], dims[dim] * dims[dim + 1], *dims[dim + 2 :])
+
+
+def gather_around(x, axis, dim):
+    length = lax.axis_size(axis)
+    pairs = [(i, (i + 1) % length) for i in range(length)]
+    back = [(b, a) for a, b in pairs]
+    lower, upper = ([], [])
+    for step in range(length - 1):
+        if step % 2 == 0:
+            lower.append(lax.ppermute(lower[-1] if lower else x, axis, pairs))
+        else:
+            upper.append(lax.ppermute(upper[-1] if upper else x, axis, back))
+    blocks = jnp.stack([*lower[::-1], x, *upper])
+    shift = lax.axis_index(axis) - len(lower)
+    blocks = blocks[(jnp.arange(length) - shift) % length]
+    return laid_out(blocks, dim)
 
 
 def from_behind(value, axis, by):
@@ -92,7 +114,7 @@
     per_group = HQ // HK
     kv_width = HK * HD
     key_full, value_full = (
-        lax.all_gather(w_key, "dp", axis=0, tiled=True),
+        gather_around(w_key, "dp", 0),
         lax.all_gather(w_value, "dp", axis=0, tiled=True),
     )
     key_own = jnp.dot(tokens, key_full, preferred_element_type=jnp.float32).astype(jnp.bfloat16)

time: 782 us -> 739 us (0.945)
  waiting for transfers between devices: 364 us -> 319 us
  local copies, waits for them, and re-layouts: 47.8 us -> 36.6 us
  starting transfers between devices: 35.8 us -> 43.9 us
    all_gather x1, waiting for transfers between devices: 37.5 us -> 0.09 us  [shards(): lax.all_gather(w_value, 'dp', axis=0, tiled=True)]
    all_gather x1 -> x0, waiting for transfers between devices: 35 us -> none  [shards(): lax.all_gather(w_key, 'dp', axis=0, tiled=True)]
    ppermute x0 -> x3, waiting for transfers between devices: none -> 35 us  [the longest x2 35 us: gather_around(): lower.append(lax.ppermute(lower[-1] if lower else x, axis, pairs))]
    reshape x3 -> x0, local copies, waits for them, and re-layouts: 11.6 us -> none  [the longest x2 9.5 us: masked_scores(): key_heads = key_rows.reshape(key_rows.shape[0], HK, HD)]
    unnamed x4 -> x3, waiting for transfers between devices: 140 us -> 134 us
    unnamed x41 -> x43, local copies, waits for them, and re-layouts: 30.9 us -> 30 us
  transfers between devices with their start and end apart: 19 -> 21, of which waited for: 10 -> 10; matrix products, arithmetic and copies ran while one was open for 3% -> 5% of each run, Pallas kernels for 0% -> 0%
where the time goes in v1:
time: 739 us; the launch traced here: 737 us
  waiting for transfers between devices  319 us (43%)
  blocking collectives  278 us (38%)
  starting transfers between devices  43.9 us (6%)
  local copies, waits for them, and re-layouts  36.6 us (5%)
  matrix products  32.1 us (4%)
  between operations  14.5 us (2%)
  other arithmetic  13.6 us (2%)
    psum x1, blocking collectives, shards(): weight_grad = lax.psum(share_sum, 'ctx').astype(jnp.bfloat16)  278 us
    ppermute x16, waiting for transfers between devices, from_behind(): return lax.ppermute(value, axis, pairs)  149 us
    unnamed x3, waiting for transfers between devices  134 us
    ppermute x16, starting transfers between devices, from_behind(): return lax.ppermute(value, axis, pairs)  39.9 us
    ppermute x2, waiting for transfers between devices, gather_around(): lower.append(lax.ppermute(lower[-1] if lower else x, axis, pairs))  35 us
    unnamed x43, local copies, waits for them, and re-layouts  30 us
  transfers between devices with their start and end apart: 21, of which 10 were waited for; matrix products, arithmetic and copies ran while one was open for 5% of the time, Pallas kernels for 0%

profile of v1, /device:TPU:2, one launch (start us, length us, event | category | flops | bytes accessed | tf_op | source)
XLA Modules:
  0.0 737.2 jit_solution(4434840999745719413)
XLA Ops:
  10.4 12.9 %collective-permute-done = bf16[576,512]{1,0:T(8,128)(2,1)S(1)} collective-permute-done((bf16[576,512]{1,0:T(8,128)(2,1)}, bf16[576,512]{1,0:T(8,128)(2,1)S(1)}, u32[]{:S(2)}, u32[]{:S(2)}) %collective-permute-start) | collective-permute-done | bytes 589856 | tf_op jit(solution)/shard_map/ppermute | solution.py:27
  27.7 22.0 %collective-permute-done.1 = bf16[576,512]{1,0:T(8,128)(2,1)S(1)} collective-permute-done((bf16[576,512]{1,0:T(8,128)(2,1)S(1)}, bf16[576,512]{1,0:T(8,128)(2,1)S(1)}, u32[]{:S(2)}, u32[]{:S(2)}) %collective-permute-start.1) | collective-permute-done | bytes 589856 | tf_op jit(solution)/shard_map/ppermute | solution.py:27
  49.7 2.8 pad_maximum_fusion
  52.5 2.5 gather_fusion
  56.6 2.7 convolution_convert_fusion.2
  61.8 5.1 collective-permute-start.3
  66.9 4.7 collective-permute-start.4
  71.6 4.0 collective-permute-start.5
  75.7 4.8 collective-permute-start.6
  80.5 5.0 collective-permute-start.7
  85.5 4.0 fusion.8
  89.5 2.0 copy.64
  91.5 2.0 copy.93
  96.1 2.8 collective-permute-start.9
  100.0 13.4 %collective-permute-done.5 = bf16[256,1024]{0,1:T(8,128)(2,1)} collective-permute-done((bf16[256,1024]{0,1:T(8,128)(2,1)}, bf16[256,1024]{0,1:T(8,128)(2,1)}, u32[]{:S(2)}, u32[]{:S(2)}) %collective-permute-start.5) | collective-permute-done | bytes 524320 | tf_op jit(solution)/shard_map/ppermute | solution.py:39
  118.2 2.0 collective-permute-done.9
  126.3 2.4 multiply_reduce_fusion
  128.7 4.4 fusion.2
  133.1 2.9 fusion.43
  143.5 54.8 %collective-permute-done.18 = f32[256,1024]{0,1:T(8,128)S(1)} collective-permute-done((f32[256,1024]{0,1:T(8,128)S(1)}, f32[256,1024]{0,1:T(8,128)S(1)}, u32[]{:S(2)}, u32[]{:S(2)}) %collective-permute-start.18) | collective-permute-done | bytes 1048608 | tf_op jit(solution)/shard_map/ppermute | solution.py:39
  199.8 17.6 %collective-permute-done.17 = f32[256,1024]{0,1:T(8,128)S(1)} collective-permute-done((f32[256,1024]{0,1:T(8,128)S(1)}, f32[256,1024]{0,1:T(8,128)S(1)}, u32[]{:S(2)}, u32[]{:S(2)}) %collective-permute-start.17) | collective-permute-done | bytes 1048608 | tf_op jit(solution)/shard_map/ppermute | solution.py:39
  221.0 60.4 %collective-permute-done.12 = f32[256,1024]{0,1:T(8,128)S(1)} collective-permute-done((f32[256,1024]{0,1:T(8,128)S(1)}, f32[256,1024]{0,1:T(8,128)S(1)}, u32[]{:S(2)}, u32[]{:S(2)}) %collective-permute-start.12) | collective-permute-done | bytes 1048608 | tf_op jit(solution)/shard_map/ppermute | solution.py:39
  282.9 5.1 convolution_bitcast_fusion
  287.9 9.6 %copy.91 = f32[2304,1024]{1,0:T(8,128)} copy(f32[2304,1024]{0,1:T(8,128)} %convolution_bitcast_fusion) | data formatting | bytes 18874368
  297.6 2.0 copy.71
  299.6 5.2 convolution_convert_fusion
  304.8 2.0 copy.72
  306.9 2.6 fusion.35
  311.4 133.8 %reduce-scatter.4.cloned.1.call-done = f32[576,1024]{1,0:T(8,128)} async-done(((f32[2304,1024]{1,0:T(8,128)}), f32[576,1024]{1,0:T(8,128)}) %reduce-scatter.4.cloned.1.call-update) | async-done | bytes 2359312
  445.2 3.2 copy.92
  448.4 277.9 %all-reduce.1 = bf16[576,1024]{0,1:T(8,128)(2,1)S(1)} all-reduce(f32[576,1024]{0,1:T(8,128)} %copy.92), channel_id=1, replica_groups=mesh['dp'=4,'ctx'=64] {'ctx'}, use_global_device_ids=true, to_apply=%region_7.8 | all-reduce | flops 589824 | bytes 3538944 | tf_op jit(solution)/shard_map/psum | solution.py:169
  727.2 2.1 copy.73
  (90 shorter events, 43.9 us)
Async XLA Ops:
  7.2 47.8 %copy-start = (bf16[1,256,2304]{2,1,0:T(8,128)(2,1)S(1)}, bf16[1,256,2304]{2,1,0:T(8,128)(2,1)}, u32[]{:S(2)}) copy-start(bf16[1,256,2304]{2,1,0:T(8,128)(2,1)} %param.6) | copy-start | bytes 3538948
  7.2 49.4 %all-gather.2.cloned.1.call-start = ((), (), s32[]{:S(2)}) async-start(), calls=%async_computation.1 | async-start | bytes 2949120 | tf_op jit(solution)/shard_map/all_gather | solution.py:118
  7.9 437.3 %reduce-scatter.4.cloned.1.call-start = ((), (), s32[]{:S(2)}) async-start(), calls=%async_computation.2 | async-start | bytes 11796480
  8.0 15.4 %collective-permute-start = (bf16[576,512]{1,0:T(8,128)(2,1)}, bf16[576,512]{1,0:T(8,128)(2,1)S(1)}, u32[]{:S(2)}, u32[]{:S(2)}) collective-permute-start(bf16[576,512]{1,0:T(8,128)(2,1)} %param.8), channel_id=1, source_target_pairs={{0,64},{64,128},{128,192},{192,0},{1,65},{65,129},{129,193},{193,1... | collective-permute-start | bytes 1769480 | tf_op jit(solution)/shard_map/ppermute | solution.py:27
  9.5 18.1 %collective-permute-start.2 = (bf16[576,512]{1,0:T(8,128)(2,1)}, bf16[576,512]{1,0:T(8,128)(2,1)S(1)}, u32[]{:S(2)}, u32[]{:S(2)}) collective-permute-start(bf16[576,512]{1,0:T(8,128)(2,1)} %param.8), channel_id=1, source_target_pairs={{64,0},{128,64},{192,128},{0,192},{65,1},{129,65},{193,129},{1,193... | collective-permute-start | bytes 1769480 | tf_op jit(solution)/shard_map/ppermute | solution.py:29
  10.4 39.3 %copy-start.13 = (s32[256]{0:T(256)}, s32[256]{0:T(256)S(1)}, u32[]{:S(2)}) copy-start(s32[256]{0:T(256)S(1)} %iota_add_fusion.1) | copy-start | bytes 3076
  23.3 26.4 %collective-permute-start.1 = (bf16[576,512]{1,0:T(8,128)(2,1)S(1)}, bf16[576,512]{1,0:T(8,128)(2,1)S(1)}, u32[]{:S(2)}, u32[]{:S(2)}) collective-permute-start(bf16[576,512]{1,0:T(8,128)(2,1)S(1)} %collective-permute-done), channel_id=1, source_target_pairs={{0,64},{64,128},{128,192},{192,0},{1,65},{65,129},{129,193},{193,1... | collective-permute-start | bytes 1769480 | tf_op jit(solution)/shard_map/ppermute | solution.py:27
  56.6 28.9 %copy-start.12 = (s32[2304]{0:T(1024)S(1)}, s32[2304]{0:T(1024)}, u32[]{:S(2)}) copy-start(s32[2304]{0:T(1024)} %convert_reduce_fusion) | copy-start | bytes 27652
  61.8 31.7 %collective-permute-start.3 = (bf16[256,1024]{0,1:T(8,128)(2,1)}, bf16[256,1024]{0,1:T(8,128)(2,1)}, u32[]{:S(2)}, u32[]{:S(2)}) collective-permute-start(bf16[256,1024]{0,1:T(8,128)(2,1)} %pad_maximum_fusion.2), channel_id=1, source_target_pairs={{0,8},{1,9},{2,10},{3,11},{4,12},{5,13},{6,14},{7,15},{8,16},{9,17... | collective-permute-start | bytes 1572872 | tf_op jit(solution)/shard_map/ppermute | solution.py:39
  66.9 29.2 %collective-permute-start.4 = (bf16[256,1024]{0,1:T(8,128)(2,1)}, bf16[256,1024]{0,1:T(8,128)(2,1)}, u32[]{:S(2)}, u32[]{:S(2)}) collective-permute-start(bf16[256,1024]{0,1:T(8,128)(2,1)} %pad_maximum_fusion.2), channel_id=1, source_target_pairs={{0,7},{1,8},{2,9},{3,10},{4,11},{5,12},{6,13},{7,14},{8,15},{9,16}... | collective-permute-start | bytes 1572872 | tf_op jit(solution)/shard_map/ppermute | solution.py:39
  71.6 41.8 %collective-permute-start.5 = (bf16[256,1024]{0,1:T(8,128)(2,1)}, bf16[256,1024]{0,1:T(8,128)(2,1)}, u32[]{:S(2)}, u32[]{:S(2)}) collective-permute-start(bf16[256,1024]{0,1:T(8,128)(2,1)} %pad_maximum_fusion.2), channel_id=1, source_target_pairs={{0,6},{1,7},{2,8},{3,9},{4,10},{5,11},{6,12},{7,13},{8,14},{9,15},... | collective-permute-start | bytes 1572872 | tf_op jit(solution)/shard_map/ppermute | solution.py:39
  75.7 40.3 %collective-permute-start.6 = (bf16[256,1024]{0,1:T(8,128)(2,1)}, bf16[256,1024]{0,1:T(8,128)(2,1)}, u32[]{:S(2)}, u32[]{:S(2)}) collective-permute-start(bf16[256,1024]{0,1:T(8,128)(2,1)} %pad_maximum_fusion.2), channel_id=1, source_target_pairs={{0,5},{1,6},{2,7},{3,8},{4,9},{5,10},{6,11},{7,12},{8,13},{9,14},{... | collective-permute-start | bytes 1572872 | tf_op jit(solution)/shard_map/ppermute | solution.py:39
  80.5 36.6 %collective-permute-start.7 = (bf16[256,1024]{0,1:T(8,128)(2,1)}, bf16[256,1024]{0,1:T(8,128)(2,1)}, u32[]{:S(2)}, u32[]{:S(2)}) collective-permute-start(bf16[256,1024]{0,1:T(8,128)(2,1)} %pad_maximum_fusion.2), channel_id=1, source_target_pairs={{0,4},{1,5},{2,6},{3,7},{4,8},{5,9},{6,10},{7,11},{8,12},{9,13},{1... | collective-permute-start | bytes 1572872 | tf_op jit(solution)/shard_map/ppermute | solution.py:39
  93.6 26.7 %copy-start.8 = (bf16[256,512]{0,1:T(8,128)(2,1)S(1)}, bf16[256,512]{0,1:T(8,128)(2,1)}, u32[]{:S(2)}) copy-start(bf16[256,512]{0,1:T(8,128)(2,1)} %fusion.15) | copy-start | bytes 786436
  93.6 26.8 %copy-start.10 = (bf16[256,512]{0,1:T(8,128)(2,1)S(1)}, bf16[256,512]{0,1:T(8,128)(2,1)}, u32[]{:S(2)}) copy-start(bf16[256,512]{0,1:T(8,128)(2,1)} %copy-done.9) | copy-start | bytes 786436
  93.6 24.6 %collective-permute-start.8 = (bf16[256,1024]{0,1:T(8,128)(2,1)}, bf16[256,1024]{0,1:T(8,128)(2,1)S(1)}, u32[]{:S(2)}, u32[]{:S(2)}) collective-permute-start(bf16[256,1024]{0,1:T(8,128)(2,1)} %pad_maximum_fusion.2), channel_id=1, source_target_pairs={{0,3},{1,4},{2,5},{3,6},{4,7},{5,8},{6,9},{7,10},{8,11},{9,12},{10... | collective-permute-start | bytes 1572872 | tf_op jit(solution)/shard_map/ppermute | solution.py:39
  96.1 24.1 %collective-permute-start.9 = (bf16[256,1024]{0,1:T(8,128)(2,1)}, bf16[256,1024]{0,1:T(8,128)(2,1)S(1)}, u32[]{:S(2)}, u32[]{:S(2)}) collective-permute-start(bf16[256,1024]{0,1:T(8,128)(2,1)} %pad_maximum_fusion.2), channel_id=1, source_target_pairs={{0,2},{1,3},{2,4},{3,5},{4,6},{5,7},{6,8},{7,9},{8,10},{9,11},{10,... | collective-permute-start | bytes 1572872 | tf_op jit(solution)/shard_map/ppermute | solution.py:39
  113.4 6.9 collective-permute-start.10
  120.4 1.2 copy-start.11
  120.7 2.8 copy-start.6
  120.7 5.6 copy-start.2
  123.6 1.3 copy-start.5
  133.1 2.9 copy-start.1
  137.0 61.3 %collective-permute-start.18 = (f32[256,1024]{0,1:T(8,128)S(1)}, f32[256,1024]{0,1:T(8,128)S(1)}, u32[]{:S(2)}, u32[]{:S(2)}) collective-permute-start(f32[256,1024]{0,1:T(8,128)S(1)} %get-tuple-element.31), channel_id=1, source_target_pairs={{8,0},{9,1},{10,2},{11,3},{12,4},{13,5},{14,6},{15,7},{16,8},{17,9... | collective-permute-start | bytes 3145736 | tf_op jit(solution)/shard_map/ppermute | solution.py:39
  138.3 79.1 %collective-permute-start.17 = (f32[256,1024]{0,1:T(8,128)S(1)}, f32[256,1024]{0,1:T(8,128)S(1)}, u32[]{:S(2)}, u32[]{:S(2)}) collective-permute-start(f32[256,1024]{0,1:T(8,128)S(1)} %get-tuple-element.32), channel_id=1, source_target_pairs={{7,0},{8,1},{9,2},{10,3},{11,4},{12,5},{13,6},{14,7},{15,8},{16,9}... | collective-permute-start | bytes 3145736 | tf_op jit(solution)/shard_map/ppermute | solution.py:39
  139.6 79.1 %collective-permute-start.16 = (f32[256,1024]{0,1:T(8,128)S(1)}, f32[256,1024]{0,1:T(8,128)S(1)}, u32[]{:S(2)}, u32[]{:S(2)}) collective-permute-start(f32[256,1024]{0,1:T(8,128)S(1)} %get-tuple-element.30), channel_id=1, source_target_pairs={{6,0},{7,1},{8,2},{9,3},{10,4},{11,5},{12,6},{13,7},{14,8},{15,9},... | collective-permute-start | bytes 3145736 | tf_op jit(solution)/shard_map/ppermute | solution.py:39
  140.9 79.1 %collective-permute-start.15 = (f32[256,1024]{0,1:T(8,128)S(1)}, f32[256,1024]{0,1:T(8,128)S(1)}, u32[]{:S(2)}, u32[]{:S(2)}) collective-permute-start(f32[256,1024]{0,1:T(8,128)S(1)} %get-tuple-element.29), channel_id=1, source_target_pairs={{5,0},{6,1},{7,2},{8,3},{9,4},{10,5},{11,6},{12,7},{13,8},{14,9},{... | collective-permute-start | bytes 3145736 | tf_op jit(solution)/shard_map/ppermute | solution.py:39
  142.2 77.8 %collective-permute-start.14 = (f32[256,1024]{0,1:T(8,128)S(1)}, f32[256,1024]{0,1:T(8,128)S(1)}, u32[]{:S(2)}, u32[]{:S(2)}) collective-permute-start(f32[256,1024]{0,1:T(8,128)S(1)} %get-tuple-element.28), channel_id=1, source_target_pairs={{4,0},{5,1},{6,2},{7,3},{8,4},{9,5},{10,6},{11,7},{12,8},{13,9},{1... | collective-permute-start | bytes 3145736 | tf_op jit(solution)/shard_map/ppermute | solution.py:39
  198.3 22.7 %collective-permute-start.13 = (f32[256,1024]{0,1:T(8,128)S(1)}, f32[256,1024]{0,1:T(8,128)S(1)}, u32[]{:S(2)}, u32[]{:S(2)}) collective-permute-start(f32[256,1024]{0,1:T(8,128)S(1)} %get-tuple-element.27), channel_id=1, source_target_pairs={{3,0},{4,1},{5,2},{6,3},{7,4},{8,5},{9,6},{10,7},{11,8},{12,9},{13... | collective-permute-start | bytes 3145736 | tf_op jit(solution)/shard_map/ppermute | solution.py:39
  217.3 64.1 %collective-permute-start.12 = (f32[256,1024]{0,1:T(8,128)S(1)}, f32[256,1024]{0,1:T(8,128)S(1)}, u32[]{:S(2)}, u32[]{:S(2)}) collective-permute-start(f32[256,1024]{0,1:T(8,128)S(1)} %get-tuple-element.26), channel_id=1, source_target_pairs={{2,0},{3,1},{4,2},{5,3},{6,4},{7,5},{8,6},{9,7},{10,8},{11,9},{12,... | collective-permute-start | bytes 3145736 | tf_op jit(solution)/shard_map/ppermute | solution.py:39
  218.6 62.8 %collective-permute-start.11 = (f32[256,1024]{0,1:T(8,128)S(1)}, f32[256,1024]{0,1:T(8,128)S(1)}, u32[]{:S(2)}, u32[]{:S(2)}) collective-permute-start(f32[256,1024]{0,1:T(8,128)S(1)} %get-tuple-element.25), channel_id=1, source_target_pairs={{1,0},{2,1},{3,2},{4,3},{5,4},{6,5},{7,6},{8,7},{9,8},{10,9},{11,1... | collective-permute-start | bytes 3145736 | tf_op jit(solution)/shard_map/ppermute | solution.py:39
  306.9 2.6 copy-start.4
  (3 other events, 2.6 us)
Sparse Core Ops, SparseCore 0:
  9.8 46.7 all-gather.1
  297.7 147.4 reduce-scatter.3
